TPU v7x, 32 devices: a whole 2x2x4 slice. The times are simulated.
32 devices in a mesh: visit: 4 (over z), row: 2 (over core), col: 4 (over y, x).
Axes of the slice: x: 2, y: 2, z: 4, core: 2. Of those that a mesh axis runs over, the one named last changes fastest.
Arguments:
- images: bfloat16 [16, 1024, 2048], P('visit', 'row', 'col'), may hold values from -10 to 10, as said below
- coeffs: float32 [16, 3], P('visit'), may hold values from 0.3 to 1.2
- pair_list: int32 [8, 3], replicated, may hold values from 0 to 480, as said below
- weights: bfloat16 [16, 2, 4], P('visit', 'row', 'col'), may hold values from 0.5 to 4
- resample_bank: bfloat16 [12, 512, 512], replicated, may hold values from -0.25 to 0.25
- warp_index: int32 [16, 2, 4, 2], P('visit', 'row', 'col'), may hold values from 0 to 11
- destinations: int32 [16, 2, 4, 4], P('visit', 'row', 'col'), may hold values from 0 to 3, as said below
- counts: int32 [16, 2, 4], P('visit', 'row', 'col'), may hold values from 3 to 4
Outputs:
- coadd_patch: float32 [4, 1024, 2048], P('visit', 'row', 'col')
- plane_fit: float32 [16, 3], P('visit')
Inputs may be any that keep to these rules, and one draw needn't show every extreme that they name: `images`: noise plus a per-exposure sky plane. `pair_list`: every exposure appears in exactly one pair; offsets lie in 0 to 480, both ends used. `destinations`: the used entries of one tile's list are distinct; each tile lists the patch of its own visit index; a patch drawn with skew, which may be the device's own visit patch, is listed by all 4 tiles at each device position.
All inputs are finite; a program needn't handle non-finite values.
Results may differ from a plain program's by a relative error of at most 0.015.
Values may be sent and summed in bfloat16 or wider, within the bound.
No kernel may reach another device: no remote copies, remote signals or barrier semaphores. Data moves between devices by JAX's collectives and lax.ppermute only.
A program may use at most 192 MiB of HBM per device.

v0:
```python
import jax
import jax.numpy as jnp
from jax import lax
from jax.sharding import PartitionSpec as P

HALO = 16
STRIP = 32
MAXD = 4
SIGMA_PARTS = (0.0625, 0.125, 0.25)


def extended(value, sides, width):
    for axis, dim in sides:
        devices, length = (lax.axis_size(axis), value.shape[dim])
        up = [(i, (i + 1) % devices) for i in range(devices - 1)]
        down = [(j, i) for i, j in up]
        last = lax.slice_in_dim(value, length - width, length, axis=dim)
        initial = lax.slice_in_dim(value, 0, width, axis=dim)
        before = lax.ppermute(last, axis, up)
        after = lax.ppermute(initial, axis, down)
        value = jnp.concatenate([before, value, after], axis=dim)
    return value


def band_table(length, width, sigma):
    spread = (jnp.arange(2 * width + 1) - width).astype(jnp.float32)
    curve = jnp.exp(-spread * spread / (2.0 * sigma * sigma))
    total = jnp.sum(curve)
    rows_grid = lax.broadcasted_iota(jnp.int32, (length, length + 2 * width), 0)
    cols_grid = lax.broadcasted_iota(jnp.int32, (length, length + 2 * width), 1)
    offset = (cols_grid - rows_grid - width).astype(jnp.float32)
    values = jnp.exp(-offset * offset / (2.0 * sigma * sigma)) / total
    return jnp.where(jnp.abs(offset) <= width, values, 0.0).astype(jnp.bfloat16)


def centred(index, length):
    return (index.astype(jnp.float32) + 0.5) / length * 2.0 - 1.0


def solve_three(normal, moments):
    lower = jnp.linalg.cholesky(normal)
    first = moments[..., 0] / lower[..., 0, 0]
    second = (moments[..., 1] - lower[..., 1, 0] * first) / lower[..., 1, 1]
    third = (moments[..., 2] - lower[..., 2, 0] * first - lower[..., 2, 1] * second) / lower[
        ..., 2, 2
    ]
    upper_top = third / lower[..., 2, 2]
    upper_mid = (second - lower[..., 2, 1] * upper_top) / lower[..., 1, 1]
    upper_low = (first - lower[..., 1, 0] * upper_mid - lower[..., 2, 0] * upper_top) / lower[
        ..., 0, 0
    ]
    return jnp.stack([upper_low, upper_mid, upper_top], -1)


def rows_from(source, anchor):
    return lax.dynamic_slice_in_dim(source, anchor, STRIP, 0)


def shards(images, coeffs, pair_list, weights, resample_bank, warp_index, destinations, counts):
    exp_dev = images.shape[0]
    tile_len = images.shape[1]
    row_count = lax.axis_size("row")
    col_count = lax.axis_size("col")
    visit_count = lax.axis_size("visit")
    row_pos = lax.axis_index("row")
    col_pos = lax.axis_index("col")
    visit_pos = lax.axis_index("visit")
    height = row_count * tile_len
    breadth = col_count * tile_len
    padded = extended(images, (("row", 1), ("col", 2)), HALO)
    matched = jnp.zeros((exp_dev, tile_len, tile_len), jnp.float32)
    for kernel in range(len(SIGMA_PARTS)):
        table = band_table(tile_len, HALO, HALO * SIGMA_PARTS[kernel])
        across = jnp.einsum(
            "ij,ejl->eil", table, padded, preferred_element_type=jnp.float32
        ).astype(jnp.bfloat16)
        smoothed = jnp.einsum("eil,ml->eim", across, table, preferred_element_type=jnp.float32)
        matched = matched + coeffs[:, kernel, None, None] * smoothed
    own_ids = visit_pos * exp_dev + jnp.arange(exp_dev, dtype=jnp.int32)
    first_col = pair_list[:, 0]
    second_col = pair_list[:, 1]
    offsets = pair_list[:, 2]
    hit_first = first_col[None, :] == own_ids[:, None]
    hit_second = second_col[None, :] == own_ids[:, None]
    partner = jnp.sum(
        jnp.where(hit_first, second_col[None, :], 0) + jnp.where(hit_second, first_col[None, :], 0),
        axis=1,
    )
    offset = jnp.sum(jnp.where(hit_first | hit_second, offsets[None, :], 0), axis=1)
    own_strip = jax.vmap(rows_from)(images, offset)
    everyone = lax.all_gather(own_strip, "visit", axis=0, tiled=True)
    theirs = jnp.take(everyone, partner, axis=0).astype(jnp.float32)
    nearby = jax.vmap(rows_from)(matched, offset)
    difference = nearby - theirs
    pixel_weight = 1.0 / (1.0 + theirs * theirs)
    strip_rows = row_pos * tile_len + offset[:, None] + jnp.arange(STRIP, dtype=jnp.int32)[None, :]
    ycoord = centred(strip_rows, height)[:, :, None]
    xcoord = centred(col_pos * tile_len + jnp.arange(tile_len, dtype=jnp.int32), breadth)
    xgrid = xcoord[None, None, :]
    weight_x = pixel_weight * xgrid
    weight_y = pixel_weight * ycoord
    sum_w = jnp.sum(pixel_weight, axis=(1, 2))
    sum_x = jnp.sum(weight_x, axis=(1, 2))
    sum_y = jnp.sum(weight_y, axis=(1, 2))
    sum_xx = jnp.sum(weight_x * xgrid, axis=(1, 2))
    sum_xy = jnp.sum(weight_x * ycoord, axis=(1, 2))
    sum_yy = jnp.sum(weight_y * ycoord, axis=(1, 2))
    normal = jnp.stack(
        [
            jnp.stack([sum_w, sum_x, sum_y], -1),
            jnp.stack([sum_x, sum_xx, sum_xy], -1),
            jnp.stack([sum_y, sum_xy, sum_yy], -1),
        ],
        1,
    )
    moments = jnp.stack(
        [
            jnp.sum(pixel_weight * difference, axis=(1, 2)),
            jnp.sum(weight_x * difference, axis=(1, 2)),
            jnp.sum(weight_y * difference, axis=(1, 2)),
        ],
        -1,
    )
    normal, moments = lax.psum((normal, moments), ("row", "col"))
    plane_fit = solve_three(normal, moments)
    row_coord = centred(row_pos * tile_len + jnp.arange(tile_len, dtype=jnp.int32), height)
    background = (
        plane_fit[:, 0, None, None]
        + plane_fit[:, 1, None, None] * xcoord[None, None, :]
        + plane_fit[:, 2, None, None] * row_coord[None, :, None]
    )
    corrected = (matched - background).astype(jnp.bfloat16)
    choose = warp_index[:, 0, 0, :]
    row_maps = jnp.take(resample_bank, choose[:, 0], axis=0)
    col_maps = jnp.take(resample_bank, choose[:, 1], axis=0)
    halfway = jnp.einsum(
        "eij,ejk->eik", row_maps, corrected, preferred_element_type=jnp.float32
    ).astype(jnp.bfloat16)
    warped = jnp.einsum(
        "eik,elk->eil", halfway, col_maps, preferred_element_type=jnp.float32
    ).astype(jnp.bfloat16)
    listed = destinations[:, 0, 0, :]
    how_many = counts[:, 0, 0]
    usable = jnp.arange(MAXD, dtype=jnp.int32)[None, :] < how_many[:, None]
    owners = jnp.arange(visit_count, dtype=jnp.int32)
    member = jnp.any(usable[:, :, None] & (listed[:, :, None] == owners[None, None, :]), axis=1)
    tile_weight = weights[:, 0, 0]
    nothing = jnp.zeros((), jnp.bfloat16)
    picked = jnp.where(member, tile_weight[:, None], nothing)
    partial_sum = jnp.einsum("ev,eij->vij", picked, warped, preferred_element_type=jnp.float32)
    partial_weight = jnp.sum(picked.astype(jnp.float32), axis=0)
    numerator, denominator = (
        lax.psum_scatter(
            partial_sum.astype(jnp.bfloat16), "visit", scatter_dimension=0, tiled=True
        ).astype(jnp.float32),
        lax.psum_scatter(
            partial_weight.astype(jnp.bfloat16), "visit", scatter_dimension=0, tiled=True
        ).astype(jnp.float32),
    )
    coadd_patch = numerator / denominator[:, None, None]
    return (coadd_patch, plane_fit)


def solution(mesh):
    in_specs = (
        P("visit", "row", "col"),
        P("visit", None),
        P(),
        P("visit", "row", "col"),
        P(),
        P("visit", "row", "col", None),
        P("visit", "row", "col", None),
        P("visit", "row", "col"),
    )
    out_specs = (P("visit", "row", "col"), P("visit", None))
    return jax.shard_map(shards, mesh=mesh, in_specs=in_specs, out_specs=out_specs, check_vma=False)
```

profile of v0, /device:TPU:0, one launch (start us, length us, event | category | flops | bytes accessed | tf_op | source)
XLA Modules:
  0.0 194.2 jit_solution(17051824752516389986)
XLA Ops:
  7.2 0.9 fusion.128
  8.1 1.0 copy.60
  9.1 2.4 %collective-permute-start = (bf16[4,16,512]{1,2,0:T(8,128)(2,1)}, bf16[4,16,512]{1,2,0:T(8,128)(2,1)S(1)}, u32[]{:S(2)}, u32[]{:S(2)}) collective-permute-start(bf16[4,16,512]{1,2,0:T(8,128)(2,1)} %copy.60), channel_id=1, source_target_pairs={{0,4},{1,5},{2,6},{3,7},{8,12},{9,13},{10,14},{11,15},{16,20},{17,... | collective-permute-start | bytes 196616 | tf_op jit(solution)/shard_map/ppermute | solution.py:19
  11.5 1.0 copy.61
  12.5 1.4 collective-permute-start.1
  13.9 4.2 %copy.62 = bf16[4,512,512]{1,2,0:T(8,128)(2,1)} copy(bf16[4,512,512]{2,1,0:T(8,128)(2,1)} %param.10) | data formatting | bytes 4194304 | tf_op args[0]
  18.7 0.6 exponential_reduce_fusion
  19.3 0.6 exponential_reduce_fusion.2
  19.9 2.9 %copy.63 = bf16[4,512,512]{2,0,1:T(4,128)(2,1)} copy(bf16[4,512,512]{2,1,0:T(8,128)(2,1)S(1)} %copy-done) | data formatting | bytes 4194304 | tf_op args[0]
  23.3 1.9 gather_fusion.1
  25.2 17.4 %all_gather.3 = bf16[16,32,512]{2,1,0:T(8,128)(2,1)S(1)} all-gather(bf16[4,32,512]{2,1,0:T(8,128)(2,1)S(1)} %copy.64), channel_id=1, replica_groups=mesh['visit'=4,'row'=2,'col'=4] {'visit'}, dimensions={0}, use_global_device_ids=true | all-gather | bytes 655360 | tf_op jit(solution)/shard_map/all_gather | solution.py:91
  42.7 4.8 %gather_fusion.3 = bf16[4,512,512]{2,1,0:T(8,128)(2,1)} fusion(bf16[12,512,512]{2,1,0:T(8,128)(2,1)} %param.14, s32[1024]{0:T(1024)S(1)} %get-tuple-element.65), kind=kCustom, calls=%fused_computation.clone | custom fusion | bytes 4194320 | tf_op jit(solution)/shard_map/jit(_take)/gather | solution.py:134
  47.5 5.0 %gather_fusion.4 = bf16[4,512,512]{2,1,0:T(8,128)(2,1)} fusion(bf16[12,512,512]{2,1,0:T(8,128)(2,1)} %param.14, s32[1024]{0:T(1024)S(1)} %get-tuple-element.64), kind=kCustom, calls=%fused_computation.1.clone | custom fusion | bytes 4194320 | tf_op jit(solution)/shard_map/jit(_take)/gather | solution.py:135
  53.3 0.9 pad_maximum_fusion.3
  54.1 3.4 %collective-permute-start.2 = (bf16[4,544,16]{1,2,0:T(8,128)(2,1)S(1)}, bf16[4,544,16]{1,2,0:T(8,128)(2,1)S(1)}, u32[]{:S(2)}, u32[]{:S(2)}) collective-permute-start(bf16[4,544,16]{1,2,0:T(8,128)(2,1)S(1)} %get-tuple-element.49), channel_id=1, source_target_pairs={{0,1},{1,2},{2,3},{4,5},{5,6},{6,7},{8,9},{9,10},{10,11},{12,13},{... | collective-permute-start | bytes 208904 | tf_op jit(solution)/shard_map/ppermute | solution.py:19
  57.5 1.5 collective-permute-start.3
  59.6 4.2 %collective-permute-done.3 = bf16[4,544,16]{1,2,0:T(8,128)(2,1)S(1)} collective-permute-done((bf16[4,544,16]{1,2,0:T(8,128)(2,1)S(1)}, bf16[4,544,16]{1,2,0:T(8,128)(2,1)S(1)}, u32[]{:S(2)}, u32[]{:S(2)}) %collective-permute-start.3) | collective-permute-done | bytes 69664 | tf_op jit(solution)/shard_map/ppermute | solution.py:20
  63.9 7.6 %fusion.2 = f32[4,512,512]{2,1,0:T(8,128)} fusion(f32[]{:T(128)} %exponential_reduce_fusion.1, bf16[4,544,16]{1,2,0:T(8,128)(2,1)S(1)} %collective-permute-done.3, bf16[4,16,512]{1,2,0:T(8,128)(2,1)} %collective-permute-done.1, bf16[4,512,512]{1,2,0:T(8,128)(2,1)S(1)} %copy-done.1, bf16[4,16,512]{1,2,0:T(8,128)(2,1)S(1)} %collective-permute-done, ...), kind=kOutput, calls=%fused_computation.10 | convolution fusion | flops 2372083712 | bytes 6561796 | tf_op jit(solution)/shard_map/eil,ml->eim/dot_general | solution.py:77
  71.4 7.7 %fusion = f32[4,512,512]{2,1,0:T(8,128)} fusion(f32[]{:T(128)} %exponential_reduce_fusion, bf16[4,544,16]{1,2,0:T(8,128)(2,1)S(1)} %collective-permute-done.3, bf16[4,16,512]{1,2,0:T(8,128)(2,1)} %collective-permute-done.1, bf16[4,512,512]{1,2,0:T(8,128)(2,1)S(1)} %copy-done.1, bf16[4,16,512]{1,2,0:T(8,128)(2,1)S(1)} %collective-permute-done, ...), kind=kOutput, calls=%fused_computation.8 | convolution fusion | flops 2372083712 | bytes 6561796 | tf_op jit(solution)/shard_map/eil,ml->eim/dot_general | solution.py:77
  79.1 9.8 %multiply_add_fusion = f32[4,512,512]{2,1,0:T(8,128)} fusion(f32[4,512,512]{2,1,0:T(8,128)} %fusion, f32[4,512,512]{2,1,0:T(8,128)} %fusion.2, f32[4]{0:T(128)S(1)} %get-tuple-element.30, f32[4]{0:T(128)S(1)} %get-tuple-element.31, f32[4]{0:T(128)S(1)} %get-tuple-element.29, f32[]{:T(128)} %exponential_reduce_fusion.2, ...), kind=kOutput, calls=%fused_computation.6 | convolution fusion | flops 2377326592 | bytes 14950452 | tf_op jit(solution)/shard_map/eil,ml->eim/dot_general | solution.py:77
  88.9 6.8 %copy.65 = f32[4,512,512]{2,0,1:T(4,128)} copy(f32[4,512,512]{2,1,0:T(8,128)} %multiply_add_fusion) | data formatting | bytes 8388608 | tf_op jit(solution)/shard_map/add | solution.py:78
  95.7 1.9 gather_fusion.2
  98.5 27.4 %all-reduce.2 = (f32[4,3,3]{1,2,0:T(4,128)S(1)}, f32[4,3]{0,1:T(4,128)S(1)}) all-reduce(f32[4,3,3]{1,2,0:T(4,128)S(1)} %pad_maximum_fusion.4, f32[4,3]{0,1:T(4,128)S(1)} %pad_maximum_fusion.5), channel_id=1, replica_groups=mesh['visit'=4,'row'=2,'col'=4] {'row','col'}, use_global_device_ids=true, to_apply=%region_16.18 | all-reduce | flops 48 | bytes 384 | tf_op jit(solution)/shard_map/psum | solution.py:124
  126.0 1.1 custom-call.4
  128.1 6.7 %fusion.22 = bf16[4,512,512]{2,1,0:T(8,128)(2,1)} fusion(bf16[4,512,512]{2,1,0:T(8,128)(2,1)} %gather_fusion.4, pred[4]{0:T(512)(128)(4,1)S(1)} %get-tuple-element.59, f32[4,512,512]{2,1,0:T(8,128)} %multiply_add_fusion, bf16[4,512,512]{2,1,0:T(8,128)(2,1)S(1)} %copy-done.2, f32[4,512]{1,0:T(4,128)S(1)} %get-tuple-element.67, ...), kind=kOutput, calls=%fused_computation.28 | convolution fusion | flops 2154823680 | bytes 10502152 | tf_op jit(solution)/shard_map/eik,elk->eil/dot_general | solution.py:139
  134.8 4.0 %fusion.27 = bf16[4,512,512]{2,0,1:T(4,128)(2,1)S(1)} fusion(bf16[4,512,512]{2,1,0:T(8,128)(2,1)} %fusion.22, pred[4,4]{1,0:T(4,128)(4,1)S(1)} %fusion.79, bf16[4]{0:T(256)(128)(2,1)S(1)} %bitcast.139), kind=kOutput, calls=%fused_computation.29 | convolution fusion | flops 9437200 | bytes 4194328 | tf_op jit(solution)/shard_map/ev,eij->vij/dot_general | solution.py:150
  138.8 1.8 copy.79
  140.7 11.5 %all-reduce.1 = bf16[4]{0:T(256)(128)(2,1)S(1)} all-reduce(bf16[4]{0:T(256)(128)(2,1)S(1)} %select_reduce_fusion.2), channel_id=3, replica_groups=mesh['visit'=4,'row'=2,'col'=4] {'visit'}, use_global_device_ids=true, to_apply=%region_21.23.clone | all-reduce | flops 4 | bytes 16
  152.8 1.2 dynamic-slice.1
  154.7 0.7 copy.80
  155.4 29.8 %reduce-scatter.2.cloned.1.call-done = bf16[1,512,512]{2,1,0:T(8,128)(2,1)} async-done(((bf16[4,512,512]{2,1,0:T(8,128)(2,1)}), bf16[1,512,512]{2,1,0:T(8,128)(2,1)}) %reduce-scatter.2.cloned.1.call-update) | async-done | bytes 524304 | tf_op jit(solution)/shard_map/reduce_scatter | solution.py:153
  185.2 2.2 %convert_divide_fusion = f32[1,512,512]{2,1,0:T(8,128)} fusion(bf16[1,512,512]{2,1,0:T(8,128)(2,1)} %reduce-scatter.2.cloned.1.call-done, f32[]{:T(128)S(6)} %convert.2), kind=kLoop, calls=%fused_computation.40 | loop fusion | flops 524288 | bytes 1572868 | tf_op jit(solution)/shard_map/div | solution.py:160
  (71 shorter events, 5.2 us)
Async XLA Ops:
  7.2 178.1 %reduce-scatter.2.cloned.1.call-start = ((), (), s32[]{:S(2)}) async-start(), calls=%async_computation.1 | async-start | bytes 2621440 | tf_op jit(solution)/shard_map/reduce_scatter | solution.py:153
  9.1 44.1 %collective-permute-start = (bf16[4,16,512]{1,2,0:T(8,128)(2,1)}, bf16[4,16,512]{1,2,0:T(8,128)(2,1)S(1)}, u32[]{:S(2)}, u32[]{:S(2)}) collective-permute-start(bf16[4,16,512]{1,2,0:T(8,128)(2,1)} %copy.60), channel_id=1, source_target_pairs={{0,4},{1,5},{2,6},{3,7},{8,12},{9,13},{10,14},{11,15},{16,20},{17,... | collective-permute-start | bytes 196616 | tf_op jit(solution)/shard_map/ppermute | solution.py:19
  12.5 7.4 %copy-start = (bf16[4,512,512]{2,1,0:T(8,128)(2,1)S(1)}, bf16[4,512,512]{2,1,0:T(8,128)(2,1)}, u32[]{:S(2)}) copy-start(bf16[4,512,512]{2,1,0:T(8,128)(2,1)} %param.10) | copy-start | bytes 6291460
  12.5 40.7 %collective-permute-start.1 = (bf16[4,16,512]{1,2,0:T(8,128)(2,1)}, bf16[4,16,512]{1,2,0:T(8,128)(2,1)}, u32[]{:S(2)}, u32[]{:S(2)}) collective-permute-start(bf16[4,16,512]{1,2,0:T(8,128)(2,1)} %copy.61), channel_id=1, source_target_pairs={{4,0},{5,1},{6,2},{7,3},{12,8},{13,9},{14,10},{15,11},{20,16},{21,... | collective-permute-start | bytes 196616 | tf_op jit(solution)/shard_map/ppermute | solution.py:20
  19.9 2.9 %copy-start.5 = (s32[8,3]{0,1:T(4,128)S(1)}, s32[8,3]{0,1:T(4,128)}, u32[]{:S(2)}) copy-start(s32[8,3]{0,1:T(4,128)} %param.12) | copy-start | bytes 292
  19.9 3.2 %copy-start.3 = (f32[4,3]{1,0:T(4,128)S(1)}, f32[4,3]{1,0:T(4,128)}, u32[]{:S(2)}) copy-start(f32[4,3]{1,0:T(4,128)} %param.11) | copy-start | bytes 148
  22.8 19.8 %copy-start.6 = (s32[4,1,1,2]{0,3,2,1:T(2,128)S(1)}, s32[4,1,1,2]{0,3,2,1:T(2,128)}, u32[]{:S(2)}) copy-start(s32[4,1,1,2]{0,3,2,1:T(2,128)} %param.15) | copy-start | bytes 100
  47.5 5.0 %copy-start.7 = (s32[4,1,1]{0,2,1:T(1,128)S(1)}, s32[4,1,1]{0,2,1:T(1,128)}, u32[]{:S(2)}) copy-start(s32[4,1,1]{0,2,1:T(1,128)} %param.17) | copy-start | bytes 52
  47.5 5.6 %copy-start.4 = (s32[4,1,1,4]{3,2,1,0:T(1,128)S(1)}, s32[4,1,1,4]{3,2,1,0:T(1,128)}, u32[]{:S(2)}) copy-start(s32[4,1,1,4]{3,2,1,0:T(1,128)} %param.16) | copy-start | bytes 196
  47.5 5.8 %copy-start.1 = (bf16[4,512,512]{1,2,0:T(8,128)(2,1)S(1)}, bf16[4,512,512]{1,2,0:T(8,128)(2,1)}, u32[]{:S(2)}) copy-start(bf16[4,512,512]{1,2,0:T(8,128)(2,1)} %copy.62) | copy-start | bytes 6291460
  54.1 5.5 %collective-permute-start.2 = (bf16[4,544,16]{1,2,0:T(8,128)(2,1)S(1)}, bf16[4,544,16]{1,2,0:T(8,128)(2,1)S(1)}, u32[]{:S(2)}, u32[]{:S(2)}) collective-permute-start(bf16[4,544,16]{1,2,0:T(8,128)(2,1)S(1)} %get-tuple-element.49), channel_id=1, source_target_pairs={{0,1},{1,2},{2,3},{4,5},{5,6},{6,7},{8,9},{9,10},{10,11},{12,13},{... | collective-permute-start | bytes 208904 | tf_op jit(solution)/shard_map/ppermute | solution.py:19
  57.5 6.3 %collective-permute-start.3 = (bf16[4,544,16]{1,2,0:T(8,128)(2,1)S(1)}, bf16[4,544,16]{1,2,0:T(8,128)(2,1)S(1)}, u32[]{:S(2)}, u32[]{:S(2)}) collective-permute-start(bf16[4,544,16]{1,2,0:T(8,128)(2,1)S(1)} %get-tuple-element.50), channel_id=1, source_target_pairs={{1,0},{2,1},{3,2},{5,4},{6,5},{7,6},{9,8},{10,9},{11,10},{13,12},{... | collective-permute-start | bytes 208904 | tf_op jit(solution)/shard_map/ppermute | solution.py:20
  95.7 32.4 %copy-start.2 = (bf16[4,512,512]{2,1,0:T(8,128)(2,1)S(1)}, bf16[4,512,512]{2,1,0:T(8,128)(2,1)}, u32[]{:S(2)}) copy-start(bf16[4,512,512]{2,1,0:T(8,128)(2,1)} %gather_fusion.3) | copy-start | bytes 6291460
  128.1 6.7 %copy-start.8 = (bf16[4,1,1]{0,2,1:T(2,128)(2,1)S(1)}, bf16[4,1,1]{0,2,1:T(2,128)(2,1)}, u32[]{:S(2)}) copy-start(bf16[4,1,1]{0,2,1:T(2,128)(2,1)} %param.13) | copy-start | bytes 28
  140.6 11.6 %copy-start.9 = (u32[32]{0:T(128)S(1)}, u32[32]{0:T(128)}, u32[]{:S(2)}) copy-start(u32[32]{0:T(128)} %constant.184) | copy-start | bytes 388
Sparse Core Ops, SparseCore 0:
  140.7 44.4 reduce-scatter.1
where the time goes:
time: 195 us; the launch traced here: 194 us
  blocking collectives  56.3 us (29%)
  local copies, waits for them, and re-layouts  36.1 us (19%)
  matrix products  35.7 us (18%)
  waiting for transfers between devices  34.7 us (18%)
  between operations  14.9 us (8%)
  starting transfers between devices  8.7 us (4%)
  other arithmetic  7.86 us (4%)
    reduce_scatter x1, waiting for transfers between devices, shards(): lax.psum_scatter(partial_sum.astype(jnp.bfloat16), 'visit', scatter_dimen...  29.8 us
    psum x1, blocking collectives, shards(): normal, moments = lax.psum((normal, moments), ('row', 'col'))  27.4 us
    dot_general x3, matrix products, shards(): jnp.einsum('eil,ml->eim', across, table, preferred_element_type=jnp.float32)  25 us
    all_gather x1, blocking collectives, shards(): everyone = lax.all_gather(own_strip, 'visit', axis=0, tiled=True)  17.4 us
    unnamed x1, blocking collectives  11.5 us
    unnamed x25, local copies, waits for them, and re-layouts  9.58 us
    add x1, local copies, waits for them, and re-layouts, shards(): matched = matched + coeffs[:, kernel, None, None] * smoothed  6.81 us
    dot_general x1, matrix products, shards(): jnp.einsum('eik,elk->eil', halfway, col_maps, preferred_element_type=jnp....  6.68 us
  transfers between devices with their start and end apart: 5, of which 3 were waited for; matrix products, arithmetic and copies ran while one was open for 13% of the time, Pallas kernels for 0%

commit v1 on v0

--- a/solution.py
+++ b/solution.py
@@ -88,7 +88,16 @@
     )
     offset = jnp.sum(jnp.where(hit_first | hit_second, offsets[None, :], 0), axis=1)
     own_strip = jax.vmap(rows_from)(images, offset)
-    everyone = lax.all_gather(own_strip, "visit", axis=0, tiled=True)
+    ways = lax.axis_size("visit")
+    up_2 = [(d, (d + 1) % ways) for d in range(ways)]
+    down_2 = [(d, (d - 1) % ways) for d in range(ways)]
+    earlier, later = ([own_strip], [own_strip])
+    for _ in range(ways // 2):
+        earlier.append(lax.ppermute(earlier[-1], "visit", up_2))
+    for _ in range((ways - 1) // 2):
+        later.append(lax.ppermute(later[-1], "visit", down_2))
+    line = jnp.concatenate([*earlier[::-1], *later[1:]], axis=0)
+    everyone = jnp.roll(line, (lax.axis_index("visit") - ways // 2) * own_strip.shape[0], axis=0)
     theirs = jnp.take(everyone, partner, axis=0).astype(jnp.float32)
     nearby = jax.vmap(rows_from)(matched, offset)
     difference = nearby - theirs

time: 195 us -> 188 us (0.964)
  blocking collectives: 56.3 us -> 37.7 us
  local copies, waits for them, and re-layouts: 36.1 us -> 40.9 us
  other arithmetic: 7.86 us -> 12.2 us
  starting transfers between devices: 8.7 us -> 12.7 us
  matrix products: 35.7 us -> 33.6 us
    all_gather x1 -> x0, blocking collectives: 17.4 us -> none  [shards(): everyone = lax.all_gather(own_strip, 'visit', axis=0, tiled=True)]
    ppermute x0 -> x3, starting transfers between devices: none -> 5.25 us  [the longest x2 3.08 us: shards(): earlier.append(lax.ppermute(earlier[-1], 'visit', up_2))]
    concatenate x0 -> x1, local copies, waits for them, and re-layouts: none -> 4.34 us  [shards(): jnp.roll(line, (lax.axis_index('visit') - ways // 2) * own_strip.shape[0]...]
    dot_general x3, matrix products: 25 us -> 22.9 us  [shards(): jnp.einsum('eil,ml->eim', across, table, preferred_element_type=jnp.float32)]
  transfers between devices with their start and end apart: 5 -> 8, of which waited for: 3 -> 3; matrix products, arithmetic and copies ran while one was open for 13% -> 29% of each run, Pallas kernels for 0% -> 0%
where the time goes in v1:
time: 188 us; the launch traced here: 187 us
  local copies, waits for them, and re-layouts  40.9 us (22%)
  blocking collectives  37.7 us (20%)
  waiting for transfers between devices  35.1 us (19%)
  matrix products  33.6 us (18%)
  between operations  14.9 us (8%)
  starting transfers between devices  12.7 us (7%)
  other arithmetic  12.2 us (6%)
    reduce_scatter x1, waiting for transfers between devices, shards(): lax.psum_scatter(partial_sum.astype(jnp.bfloat16), 'visit', scatter_dimen...  29.8 us
    psum x1, blocking collectives, shards(): normal, moments = lax.psum((normal, moments), ('row', 'col'))  27.4 us
    dot_general x3, matrix products, shards(): jnp.einsum('eil,ml->eim', across, table, preferred_element_type=jnp.float32)  22.9 us
    unnamed x1, blocking collectives  10.4 us
    unnamed x25, local copies, waits for them, and re-layouts  9.63 us
    add x1, local copies, waits for them, and re-layouts, shards(): matched = matched + coeffs[:, kernel, None, None] * smoothed  6.81 us
    dot_general x1, matrix products, shards(): jnp.einsum('eik,elk->eil', halfway, col_maps, preferred_element_type=jnp....  6.69 us
    gather x1, local copies, waits for them, and re-layouts, shards(): col_maps = jnp.take(resample_bank, choose[:, 1], axis=0)  5.01 us
  transfers between devices with their start and end apart: 8, of which 3 were waited for; matrix products, arithmetic and copies ran while one was open for 29% of the time, Pallas kernels for 0%

profile of v1, /device:TPU:0, one launch (start us, length us, event | category | flops | bytes accessed | tf_op | source)
XLA Modules:
  0.0 187.4 jit_solution(16250705962476256282)
XLA Ops:
  7.2 0.8 slice_bitcast_fusion
  8.2 4.7 %copy.63 = bf16[4,512,512]{2,0,1:T(4,128)(2,1)} copy(bf16[4,512,512]{2,1,0:T(8,128)(2,1)} %param.10) | data formatting | bytes 4194304 | tf_op args[0]
  12.9 1.9 gather_fusion.1
  14.8 3.1 %collective-permute-start.4 = (bf16[4,32,512]{2,0,1:T(4,128)(2,1)S(1)}, bf16[4,32,512]{2,0,1:T(4,128)(2,1)}, u32[]{:S(2)}, u32[]{:S(2)}) collective-permute-start(bf16[4,32,512]{2,0,1:T(4,128)(2,1)S(1)} %gather_fusion.1), channel_id=1, source_target_pairs={{0,8},{8,16},{16,24},{24,0},{1,9},{9,17},{17,25},{25,1},{2,10},{10... | collective-permute-start | bytes 393224 | tf_op jit(solution)/shard_map/ppermute | solution.py:96
  17.9 2.2 %collective-permute-start.6 = (bf16[4,32,512]{2,0,1:T(4,128)(2,1)S(1)}, bf16[4,32,512]{2,0,1:T(4,128)(2,1)}, u32[]{:S(2)}, u32[]{:S(2)}) collective-permute-start(bf16[4,32,512]{2,0,1:T(4,128)(2,1)S(1)} %gather_fusion.1), channel_id=1, source_target_pairs={{0,24},{8,0},{16,8},{24,16},{1,25},{9,1},{17,9},{25,17},{2,26},{10... | collective-permute-start | bytes 393224 | tf_op jit(solution)/shard_map/ppermute | solution.py:98
  20.1 1.0 copy.60
  21.1 1.5 collective-permute-start
  22.6 1.0 copy.61
  23.6 1.3 collective-permute-start.1
  24.9 2.4 %copy.62 = bf16[4,512,512]{1,2,0:T(8,128)(2,1)} copy(bf16[4,512,512]{2,1,0:T(8,128)(2,1)S(1)} %copy-done) | data formatting | bytes 4194304 | tf_op args[0]
  31.2 4.8 %gather_fusion.3 = bf16[4,512,512]{2,1,0:T(8,128)(2,1)} fusion(bf16[12,512,512]{2,1,0:T(8,128)(2,1)} %param.14, s32[1024]{0:T(1024)S(1)} %get-tuple-element.65), kind=kCustom, calls=%fused_computation.clone | custom fusion | bytes 4194320 | tf_op jit(solution)/shard_map/jit(_take)/gather | solution.py:143
  36.0 5.0 %gather_fusion.4 = bf16[4,512,512]{2,1,0:T(8,128)(2,1)} fusion(bf16[12,512,512]{2,1,0:T(8,128)(2,1)} %param.14, s32[1024]{0:T(1024)S(1)} %get-tuple-element.64), kind=kCustom, calls=%fused_computation.1.clone | custom fusion | bytes 4194320 | tf_op jit(solution)/shard_map/jit(_take)/gather | solution.py:144
  42.3 3.4 %collective-permute-start.2 = (bf16[4,544,16]{1,2,0:T(8,128)(2,1)S(1)}, bf16[4,544,16]{1,2,0:T(8,128)(2,1)S(1)}, u32[]{:S(2)}, u32[]{:S(2)}) collective-permute-start(bf16[4,544,16]{1,2,0:T(8,128)(2,1)S(1)} %get-tuple-element.49), channel_id=1, source_target_pairs={{0,1},{1,2},{2,3},{4,5},{5,6},{6,7},{8,9},{9,10},{10,11},{12,13},{... | collective-permute-start | bytes 208904 | tf_op jit(solution)/shard_map/ppermute | solution.py:19
  45.7 1.3 collective-permute-start.3
  47.5 0.8 collective-permute-done.2
  48.3 4.5 %collective-permute-done.3 = bf16[4,544,16]{1,2,0:T(8,128)(2,1)S(1)} collective-permute-done((bf16[4,544,16]{1,2,0:T(8,128)(2,1)S(1)}, bf16[4,544,16]{1,2,0:T(8,128)(2,1)S(1)}, u32[]{:S(2)}, u32[]{:S(2)}) %collective-permute-start.3) | collective-permute-done | bytes 69664 | tf_op jit(solution)/shard_map/ppermute | solution.py:20
  52.8 6.6 %fusion.2 = f32[4,512,512]{2,1,0:T(8,128)} fusion(f32[]{:T(128)} %exponential_reduce_fusion.1, bf16[4,544,16]{1,2,0:T(8,128)(2,1)S(1)} %collective-permute-done.3, bf16[4,16,512]{1,2,0:T(8,128)(2,1)S(1)} %collective-permute-done.1, bf16[4,512,512]{1,2,0:T(8,128)(2,1)S(1)} %copy-done.1, bf16[4,16,512]{1,2,0:T(8,128)(2,1)S(1)} %collective-permute-done, ...), kind=kOutput, calls=%fused_computation.10 | convolution fusion | flops 2372083712 | bytes 6561796 | tf_op jit(solution)/shard_map/eil,ml->eim/dot_general | solution.py:77
  59.4 6.6 %fusion = f32[4,512,512]{2,1,0:T(8,128)} fusion(f32[]{:T(128)} %exponential_reduce_fusion, bf16[4,544,16]{1,2,0:T(8,128)(2,1)S(1)} %collective-permute-done.3, bf16[4,16,512]{1,2,0:T(8,128)(2,1)S(1)} %collective-permute-done.1, bf16[4,512,512]{1,2,0:T(8,128)(2,1)S(1)} %copy-done.1, bf16[4,16,512]{1,2,0:T(8,128)(2,1)S(1)} %collective-permute-done, ...), kind=kOutput, calls=%fused_computation.8 | convolution fusion | flops 2372083712 | bytes 6561796 | tf_op jit(solution)/shard_map/eil,ml->eim/dot_general | solution.py:77
  66.0 9.7 %multiply_add_fusion = f32[4,512,512]{2,1,0:T(8,128)} fusion(f32[4,512,512]{2,1,0:T(8,128)} %fusion, f32[4,512,512]{2,1,0:T(8,128)} %fusion.2, f32[4]{0:T(128)S(1)} %get-tuple-element.30, f32[4]{0:T(128)S(1)} %get-tuple-element.31, f32[4]{0:T(128)S(1)} %get-tuple-element.29, f32[]{:T(128)} %exponential_reduce_fusion.2, ...), kind=kOutput, calls=%fused_computation.6 | convolution fusion | flops 2377326592 | bytes 14950452 | tf_op jit(solution)/shard_map/eil,ml->eim/dot_general | solution.py:77
  75.8 6.8 %copy.65 = f32[4,512,512]{2,0,1:T(4,128)} copy(f32[4,512,512]{2,1,0:T(8,128)} %multiply_add_fusion) | data formatting | bytes 8388608 | tf_op jit(solution)/shard_map/add | solution.py:78
  82.6 1.9 %gather_fusion.2 = f32[4,32,512]{2,0,1:T(4,128)S(1)} fusion(f32[4,512,512]{2,0,1:T(4,128)} %copy.65, s32[4]{0:T(128)S(1)} %fusion.95), kind=kCustom, calls=%fused_computation.4 | custom fusion | bytes 524336 | tf_op jit(solution)/shard_map/vmap()/gather | solution.py:56
  84.5 4.3 %concatenate.19 = bf16[32,32,512]{2,0,1:T(8,128)(2,1)S(1)} concatenate(bf16[4,32,512]{2,0,1:T(4,128)(2,1)} %collective-permute-done.5, bf16[4,32,512]{2,0,1:T(4,128)(2,1)} %collective-permute-done.4, bf16[4,32,512]{2,0,1:T(4,128)(2,1)S(1)} %gather_fusion.1, bf16[4,32,512]{2,0,1:T(4,128)(2,1)} %collective-permute-done.6, bf16[4,32,512]{2,0,1:T(4,128)(2,1)} %collective-permute-done.5, ...), dimensions={0} | concatenate | bytes 2097152 | tf_op jit(solution)/shard_map/jit(_roll_dynamic)/concatenate | solution.py:100
  90.0 1.1 multiply_reduce_fusion.5
  91.5 27.4 %all-reduce.2 = (f32[4,3,3]{1,2,0:T(4,128)S(1)}, f32[4,3]{0,1:T(4,128)S(1)}) all-reduce(f32[4,3,3]{1,2,0:T(4,128)S(1)} %pad_maximum_fusion.4, f32[4,3]{0,1:T(4,128)S(1)} %pad_maximum_fusion.5), channel_id=1, replica_groups=mesh['visit'=4,'row'=2,'col'=4] {'row','col'}, use_global_device_ids=true, to_apply=%region_16.18 | all-reduce | flops 48 | bytes 384 | tf_op jit(solution)/shard_map/psum | solution.py:133
  119.0 1.1 custom-call.4
  122.4 6.7 %fusion.22 = bf16[4,512,512]{2,1,0:T(8,128)(2,1)} fusion(bf16[4,512,512]{2,1,0:T(8,128)(2,1)} %gather_fusion.4, pred[4]{0:T(512)(128)(4,1)} %get-tuple-element.59, f32[4,512,512]{2,1,0:T(8,128)} %multiply_add_fusion, bf16[4,512,512]{2,1,0:T(8,128)(2,1)S(1)} %copy-done.2, f32[4,512]{1,0:T(4,128)S(1)} %get-tuple-element.67, ...), kind=kOutput, calls=%fused_computation.28 | convolution fusion | flops 2154823680 | bytes 10502152 | tf_op jit(solution)/shard_map/eik,elk->eil/dot_general | solution.py:148
  129.1 4.0 %fusion.27 = bf16[4,512,512]{2,0,1:T(4,128)(2,1)S(1)} fusion(bf16[4,512,512]{2,1,0:T(8,128)(2,1)} %fusion.22, pred[4,4]{1,0:T(4,128)(4,1)S(1)} %copy-done.6, bf16[4]{0:T(256)(128)(2,1)S(1)} %bitcast.139), kind=kOutput, calls=%fused_computation.29 | convolution fusion | flops 9437200 | bytes 4194328 | tf_op jit(solution)/shard_map/ev,eij->vij/dot_general | solution.py:159
  133.1 1.8 copy.79
  135.0 10.4 %all-reduce.1 = bf16[4]{0:T(256)(128)(2,1)S(1)} all-reduce(bf16[4]{0:T(256)(128)(2,1)S(1)} %select_reduce_fusion.2), channel_id=3, replica_groups=mesh['visit'=4,'row'=2,'col'=4] {'visit'}, use_global_device_ids=true, to_apply=%region_21.23.clone | all-reduce | flops 4 | bytes 16
  145.9 1.2 dynamic-slice.1
  148.5 29.8 %reduce-scatter.2.cloned.1.call-done = bf16[1,512,512]{2,1,0:T(8,128)(2,1)} async-done(((bf16[4,512,512]{2,1,0:T(8,128)(2,1)}), bf16[1,512,512]{2,1,0:T(8,128)(2,1)}) %reduce-scatter.2.cloned.1.call-update) | async-done | bytes 524304 | tf_op jit(solution)/shard_map/reduce_scatter | solution.py:162
  178.3 2.2 %convert_divide_fusion = f32[1,512,512]{2,1,0:T(8,128)} fusion(bf16[1,512,512]{2,1,0:T(8,128)(2,1)} %reduce-scatter.2.cloned.1.call-done, f32[]{:T(128)S(6)} %convert.2), kind=kLoop, calls=%fused_computation.40 | loop fusion | flops 524288 | bytes 1572868 | tf_op jit(solution)/shard_map/div | solution.py:169
  (78 shorter events, 11.3 us)
Async XLA Ops:
  7.2 171.2 %reduce-scatter.2.cloned.1.call-start = ((), (), s32[]{:S(2)}) async-start(), calls=%async_computation.1 | async-start | bytes 2621440 | tf_op jit(solution)/shard_map/reduce_scatter | solution.py:162
  8.2 11.8 %copy-start = (bf16[4,512,512]{2,1,0:T(8,128)(2,1)S(1)}, bf16[4,512,512]{2,1,0:T(8,128)(2,1)}, u32[]{:S(2)}) copy-start(bf16[4,512,512]{2,1,0:T(8,128)(2,1)} %param.10) | copy-start | bytes 6291460
  14.8 32.7 %collective-permute-start.4 = (bf16[4,32,512]{2,0,1:T(4,128)(2,1)S(1)}, bf16[4,32,512]{2,0,1:T(4,128)(2,1)}, u32[]{:S(2)}, u32[]{:S(2)}) collective-permute-start(bf16[4,32,512]{2,0,1:T(4,128)(2,1)S(1)} %gather_fusion.1), channel_id=1, source_target_pairs={{0,8},{8,16},{16,24},{24,0},{1,9},{9,17},{17,25},{25,1},{2,10},{10... | collective-permute-start | bytes 393224 | tf_op jit(solution)/shard_map/ppermute | solution.py:96
  17.9 66.6 %collective-permute-start.6 = (bf16[4,32,512]{2,0,1:T(4,128)(2,1)S(1)}, bf16[4,32,512]{2,0,1:T(4,128)(2,1)}, u32[]{:S(2)}, u32[]{:S(2)}) collective-permute-start(bf16[4,32,512]{2,0,1:T(4,128)(2,1)S(1)} %gather_fusion.1), channel_id=1, source_target_pairs={{0,24},{8,0},{16,8},{24,16},{1,25},{9,1},{17,9},{25,17},{2,26},{10... | collective-permute-start | bytes 393224 | tf_op jit(solution)/shard_map/ppermute | solution.py:98
  21.1 21.1 %collective-permute-start = (bf16[4,16,512]{1,2,0:T(8,128)(2,1)}, bf16[4,16,512]{1,2,0:T(8,128)(2,1)S(1)}, u32[]{:S(2)}, u32[]{:S(2)}) collective-permute-start(bf16[4,16,512]{1,2,0:T(8,128)(2,1)} %copy.60), channel_id=1, source_target_pairs={{0,4},{1,5},{2,6},{3,7},{8,12},{9,13},{10,14},{11,15},{16,20},{17,... | collective-permute-start | bytes 196616 | tf_op jit(solution)/shard_map/ppermute | solution.py:19
  23.6 18.6 %collective-permute-start.1 = (bf16[4,16,512]{1,2,0:T(8,128)(2,1)}, bf16[4,16,512]{1,2,0:T(8,128)(2,1)S(1)}, u32[]{:S(2)}, u32[]{:S(2)}) collective-permute-start(bf16[4,16,512]{1,2,0:T(8,128)(2,1)} %copy.61), channel_id=1, source_target_pairs={{4,0},{5,1},{6,2},{7,3},{12,8},{13,9},{14,10},{15,11},{20,16},{21,... | collective-permute-start | bytes 196616 | tf_op jit(solution)/shard_map/ppermute | solution.py:20
  24.9 5.5 %copy-start.3 = (f32[4,3]{1,0:T(4,128)S(1)}, f32[4,3]{1,0:T(4,128)}, u32[]{:S(2)}) copy-start(f32[4,3]{1,0:T(4,128)} %param.11) | copy-start | bytes 148
  24.9 5.7 %copy-start.5 = (s32[4,1,1,2]{0,3,2,1:T(2,128)S(1)}, s32[4,1,1,2]{0,3,2,1:T(2,128)}, u32[]{:S(2)}) copy-start(s32[4,1,1,2]{0,3,2,1:T(2,128)} %param.15) | copy-start | bytes 100
  35.9 5.0 %copy-start.7 = (s32[4,1,1]{0,2,1:T(1,128)S(1)}, s32[4,1,1]{0,2,1:T(1,128)}, u32[]{:S(2)}) copy-start(s32[4,1,1]{0,2,1:T(1,128)} %param.17) | copy-start | bytes 52
  35.9 5.1 %copy-start.4 = (s32[4,1,1,4]{3,2,1,0:T(1,128)S(1)}, s32[4,1,1,4]{3,2,1,0:T(1,128)}, u32[]{:S(2)}) copy-start(s32[4,1,1,4]{3,2,1,0:T(1,128)} %param.16) | copy-start | bytes 196
  35.9 6.2 %copy-start.1 = (bf16[4,512,512]{1,2,0:T(8,128)(2,1)S(1)}, bf16[4,512,512]{1,2,0:T(8,128)(2,1)}, u32[]{:S(2)}) copy-start(bf16[4,512,512]{1,2,0:T(8,128)(2,1)} %copy.62) | copy-start | bytes 6291460
  42.3 6.0 %collective-permute-start.2 = (bf16[4,544,16]{1,2,0:T(8,128)(2,1)S(1)}, bf16[4,544,16]{1,2,0:T(8,128)(2,1)S(1)}, u32[]{:S(2)}, u32[]{:S(2)}) collective-permute-start(bf16[4,544,16]{1,2,0:T(8,128)(2,1)S(1)} %get-tuple-element.49), channel_id=1, source_target_pairs={{0,1},{1,2},{2,3},{4,5},{5,6},{6,7},{8,9},{9,10},{10,11},{12,13},{... | collective-permute-start | bytes 208904 | tf_op jit(solution)/shard_map/ppermute | solution.py:19
  45.7 7.1 %collective-permute-start.3 = (bf16[4,544,16]{1,2,0:T(8,128)(2,1)S(1)}, bf16[4,544,16]{1,2,0:T(8,128)(2,1)S(1)}, u32[]{:S(2)}, u32[]{:S(2)}) collective-permute-start(bf16[4,544,16]{1,2,0:T(8,128)(2,1)S(1)} %get-tuple-element.50), channel_id=1, source_target_pairs={{1,0},{2,1},{3,2},{5,4},{6,5},{7,6},{9,8},{10,9},{11,10},{13,12},{... | collective-permute-start | bytes 208904 | tf_op jit(solution)/shard_map/ppermute | solution.py:20
  47.5 37.0 %collective-permute-start.5 = (bf16[4,32,512]{2,0,1:T(4,128)(2,1)}, bf16[4,32,512]{2,0,1:T(4,128)(2,1)}, u32[]{:S(2)}, u32[]{:S(2)}) collective-permute-start(bf16[4,32,512]{2,0,1:T(4,128)(2,1)} %collective-permute-done.4), channel_id=1, source_target_pairs={{0,8},{8,16},{16,24},{24,0},{1,9},{9,17},{17,25},{25,1},{2,10},{10... | collective-permute-start | bytes 393224 | tf_op jit(solution)/shard_map/ppermute | solution.py:96
  84.5 37.9 %copy-start.2 = (bf16[4,512,512]{2,1,0:T(8,128)(2,1)S(1)}, bf16[4,512,512]{2,1,0:T(8,128)(2,1)}, u32[]{:S(2)}) copy-start(bf16[4,512,512]{2,1,0:T(8,128)(2,1)} %gather_fusion.3) | copy-start | bytes 6291460
  122.4 6.7 %copy-start.6 = (pred[4,4]{1,0:T(4,128)(4,1)S(1)}, pred[4,4]{1,0:T(4,128)(4,1)}, u32[]{:S(2)}) copy-start(pred[4,4]{1,0:T(4,128)(4,1)} %fusion.79) | copy-start | bytes 52
  122.4 6.7 %copy-start.8 = (bf16[4,1,1]{0,2,1:T(2,128)(2,1)S(1)}, bf16[4,1,1]{0,2,1:T(2,128)(2,1)}, u32[]{:S(2)}) copy-start(bf16[4,1,1]{0,2,1:T(2,128)(2,1)} %param.13) | copy-start | bytes 28
  134.8 10.5 %copy-start.9 = (u32[32]{0:T(128)S(1)}, u32[32]{0:T(128)}, u32[]{:S(2)}) copy-start(u32[32]{0:T(128)} %constant.206) | copy-start | bytes 388
Sparse Core Ops, SparseCore 0:
  135.0 43.3 reduce-scatter.1
